TPU v7x, 256 devices: a whole 4x4x8 slice. The times are simulated.
256 devices in a mesh: grp: 32 (over z, x), tp: 8 (over y, core).
Axes of the slice: x: 4, y: 4, z: 8, core: 2. Of those that a mesh axis runs over, the one named last changes fastest.
Arguments:
- tokens: bfloat16 [32768, 2048], P('grp'), may hold values from -6 to 6
- norm_gain: float32 [2048], replicated, may hold values from 0.5 to 7
- w_qkv: bfloat16 [2048, 3, 2048], P(None, None, 'tp'), may hold values from -0.125 to 0.125
- w_out: bfloat16 [2048, 2048], P('tp'), may hold values from -0.125 to 0.125
- a_in: bfloat16 [64, 2048, 48], P('grp', 'tp'), may hold values from -0.125 to 0.125
- b_in: bfloat16 [64, 3, 16, 2048], P('grp', None, None, 'tp'), may hold values from -1.5 to 1.5
- a_out: bfloat16 [64, 2048, 16], P('grp', 'tp'), may hold values from -0.125 to 0.125
- b_out: bfloat16 [64, 16, 2048], P('grp', None, 'tp'), may hold values from -1.5 to 1.5
- req_len: int32 [32, 4], replicated, may hold values from 1 to 512, 1024 in all within a row
- req_adapter: int32 [32, 4], replicated, may hold values from 0 to 63, as said below
- holder: int32 [64], replicated, may hold values from 0 to 63, each once
- page_table: int32 [32, 8], P('grp'), may hold values from 0 to 7, each once within a row
Outputs:
- layer_out: bfloat16 [32768, 2048], P('grp', 'tp')
- kv_pages: bfloat16 [256, 2, 128, 2048], P('grp', None, None, 'tp')
Inputs may be any that keep to these rules, and one draw needn't show every extreme that they name: `req_adapter`: exactly 16 different adapters appear among all requests.
All inputs are finite; a program needn't handle non-finite values.
Results may differ from a plain program's by a relative error of at most 0.017.
The roundings to bfloat16 on the way count: a program that leaves them out, or rounds other values in their place, can miss the bound.
Values may be sent and summed in bfloat16 or wider, within the bound.
No kernel may reach another device: no remote copies, remote signals or barrier semaphores. Data moves between devices by JAX's collectives and lax.ppermute only.
A program may use at most 128 MiB of HBM per device.

v0:
```python
import math

import jax
import jax.numpy as jnp
from jax import lax
from jax.sharding import PartitionSpec as P

HD = 128
PAGE = 128


EPSILON = 1e-05
THETA = 10000.0


def shifted(block, axis, distance):
    devices = range(lax.axis_size(axis))
    route = [(i - distance, i) for i in devices if i - distance in devices]
    return lax.ppermute(block, axis, route)


def rms_norm(token_rows, norm_gain):
    values = token_rows.astype(jnp.float32)
    norm_scale = lax.rsqrt(jnp.mean(values * values, axis=-1, keepdims=True) + EPSILON)
    return (values * norm_scale * norm_gain).astype(jnp.bfloat16)


def request_layout(lengths, offset, tok_count):
    end_at = jnp.cumsum(lengths)
    starts = end_at - lengths
    row_ids = jnp.arange(tok_count, dtype=jnp.int32)
    segment = jnp.sum((row_ids[:, None] >= end_at[None, :]).astype(jnp.int32), axis=1)
    member = segment[:, None] == jnp.arange(lengths.shape[0], dtype=jnp.int32)[None, :]
    begin_at = jnp.sum(jnp.where(member, starts[None, :], 0), axis=1)
    position = row_ids - begin_at + jnp.where(segment == 0, offset, 0)
    return (segment, member, position)


def rotate(head_rows, position, head_dim):
    half_dim = head_dim // 2
    frequency = THETA ** (-(jnp.arange(half_dim, dtype=jnp.float32) * (2.0 / head_dim)))
    angles = position.astype(jnp.float32)[:, None] * frequency[None, :]
    cosine = jnp.cos(angles)[:, None, :]
    sine_part = jnp.sin(angles)[:, None, :]
    lower_half = head_rows[..., :half_dim]
    upper_half = head_rows[..., half_dim:]
    return jnp.concatenate(
        [
            lower_half * cosine - upper_half * sine_part,
            upper_half * cosine + lower_half * sine_part,
        ],
        axis=-1,
    )


def local(
    tokens,
    norm_gain,
    w_qkv,
    w_out,
    a_in,
    b_in,
    a_out,
    b_out,
    req_len,
    req_adapter,
    holder,
    page_table,
):
    tok_count = tokens.shape[0]
    local_width = w_out.shape[0]
    local_heads = local_width // HD
    req_count = req_len.shape[1]
    rank_dim = a_out.shape[2]
    group_id = lax.axis_index("grp")
    tp_id = lax.axis_index("tp")
    lengths = lax.dynamic_index_in_dim(req_len, group_id, 0, keepdims=False)
    earlier = lax.dynamic_index_in_dim(req_len, jnp.maximum(group_id - 1, 0), 0, keepdims=False)
    continued = group_id > 0
    prev_len = earlier[req_count - 1]
    offset = jnp.where(continued, prev_len, 0)
    segment, member, position = request_layout(lengths, offset, tok_count)
    wanted = lax.dynamic_index_in_dim(req_adapter, group_id, 0, keepdims=False)
    stacks = (
        lax.all_gather(a_in, "grp", axis=0, tiled=True),
        lax.all_gather(b_in, "grp", axis=0, tiled=True),
        lax.all_gather(a_out, "grp", axis=0, tiled=True),
        lax.all_gather(b_out, "grp", axis=0, tiled=True),
    )
    req_slots = holder[wanted]
    sel_in = jnp.take(stacks[0], req_slots, axis=0)
    sel_up = jnp.take(stacks[1], req_slots, axis=0)
    sel_odown = jnp.take(stacks[2], req_slots, axis=0)
    sel_oup = jnp.take(stacks[3], req_slots, axis=0)
    member_f = member.astype(jnp.float32)
    pick_bf = member.astype(jnp.bfloat16)
    normed = rms_norm(tokens, norm_gain)
    own_cols = lax.dynamic_slice_in_dim(normed, tp_id * local_width, local_width, 1)
    down_f = jnp.einsum("td,rdk->trk", own_cols, sel_in, preferred_element_type=jnp.float32)
    lowrank_f = lax.psum(jnp.sum(down_f * member_f[:, :, None], axis=1), "tp")
    lowrank = lowrank_f.astype(jnp.bfloat16)
    spread = (pick_bf[:, :, None] * lowrank[:, None, :]).reshape(tok_count, req_count, 3, rank_dim)
    delta_qkv = jnp.einsum("trck,rckd->tcd", spread, sel_up, preferred_element_type=jnp.float32)
    base_qkv = jnp.dot(
        normed, w_qkv.reshape(w_qkv.shape[0], 3 * local_width), preferred_element_type=jnp.float32
    )
    qkv = (base_qkv.reshape(tok_count, 3, local_width) + delta_qkv).reshape(
        tok_count, 3, local_heads, HD
    )
    query_rows = rotate(qkv[:, 0], position, HD).astype(jnp.bfloat16)
    key_rows = rotate(qkv[:, 1], position, HD).astype(jnp.bfloat16).reshape(tok_count, local_width)
    value_rows = qkv[:, 2].astype(jnp.bfloat16).reshape(tok_count, local_width)
    row_ids = jnp.arange(tok_count, dtype=jnp.int32)
    far_key, far_value = shifted((key_rows, value_rows), "grp", 1)
    far_ok = continued & (segment[:, None] == 0) & (row_ids[None, :] >= tok_count - prev_len)
    far_count = far_key.shape[0]
    near_ok = (segment[:, None] == segment[None, :]) & (row_ids[None, :] <= row_ids[:, None])
    allowed = jnp.concatenate([far_ok, near_ok], axis=1)
    key_all = jnp.concatenate([far_key, key_rows], axis=0).reshape(
        far_count + tok_count, local_heads, HD
    )
    value_all = jnp.concatenate([far_value, value_rows], axis=0).reshape(
        far_count + tok_count, local_heads, HD
    )
    score_scale = 1.0 / math.sqrt(HD)
    scores = (
        jnp.einsum("thd,shd->hts", query_rows, key_all, preferred_element_type=jnp.float32)
        * score_scale
    )
    scores = jnp.where(allowed[None], scores, -jnp.inf)
    row_top = jnp.max(scores, axis=-1, keepdims=True)
    weights = jnp.exp(scores - row_top)
    weights_bf = (weights / jnp.sum(weights, axis=-1, keepdims=True)).astype(jnp.bfloat16)
    mixed_heads = jnp.einsum(
        "hts,shd->thd", weights_bf, value_all, preferred_element_type=jnp.float32
    )
    attended = mixed_heads.astype(jnp.bfloat16).reshape(tok_count, local_width)
    partial_value = jnp.dot(attended, w_out, preferred_element_type=jnp.float32)
    base_out = lax.psum_scatter(
        partial_value.astype(jnp.bfloat16), "tp", scatter_dimension=1, tiled=True
    ).astype(jnp.float32)
    down_o = jnp.einsum("td,rdk->trk", attended, sel_odown, preferred_element_type=jnp.float32)
    low_o = lax.psum(jnp.sum(down_o * member_f[:, :, None], axis=1).astype(jnp.bfloat16), "tp")
    spread_o = (pick_bf[:, :, None] * low_o[:, None, :]).reshape(tok_count, req_count * rank_dim)
    delta_o = jnp.dot(
        spread_o,
        sel_oup.reshape(req_count * rank_dim, local_width),
        preferred_element_type=jnp.float32,
    )
    own_rows = lax.dynamic_slice_in_dim(tokens, tp_id * local_width, local_width, 1).astype(
        jnp.float32
    )
    layer_out = (own_rows + base_out + delta_o).astype(jnp.bfloat16)
    page_row = page_table[0]
    page_count = page_row.shape[0]
    numbers = jnp.arange(page_count, dtype=jnp.int32)
    inverse = jnp.sum(jnp.where(page_row[:, None] == numbers[None, :], numbers[:, None], 0), axis=0)
    both_blocks = jnp.stack(
        [
            key_rows.reshape(page_count, PAGE, local_width),
            value_rows.reshape(page_count, PAGE, local_width),
        ],
        axis=1,
    )
    kv_pages = jnp.take(both_blocks, inverse, axis=0)
    return (layer_out, kv_pages)


def solution(mesh):
    return jax.shard_map(
        local,
        mesh=mesh,
        in_specs=(
            P("grp", None),
            P(),
            P(None, None, "tp"),
            P("tp", None),
            P("grp", "tp", None),
            P("grp", None, None, "tp"),
            P("grp", "tp", None),
            P("grp", None, "tp"),
            P(),
            P(),
            P(),
            P("grp", None),
        ),
        out_specs=(P("grp", "tp"), P("grp", None, None, "tp")),
        check_vma=False,
    )
```

profile of v0, /device:TPU:2, one launch (start us, length us, event | category | flops | bytes accessed | tf_op | source)
XLA Modules:
  0.0 358.6 jit_solution(400273009174848627)
XLA Ops:
  13.9 3.1 fusion.2
  17.6 4.7 %copy.40 = bf16[2048,3,256]{0,2,1:T(8,128)(2,1)} copy(bf16[2048,3,256]{2,0,1:T(8,128)(2,1)} %param.14) | data formatting | bytes 6291456 | tf_op args[2]
  22.3 3.0 multiply_cosine_fusion
  27.9 1.9 copy-done.3
  29.8 5.1 %fusion.9 = f32[1024,3,256]{0,2,1:T(8,128)} fusion(bf16[1024,2048]{1,0:T(8,128)(2,1)S(1)} %fusion.4, bf16[2048,3,256]{0,2,1:T(8,128)(2,1)S(1)} %copy-done.5), kind=kOutput, calls=%fused_computation.21 | convolution fusion | flops 3221225472 | bytes 10485760 | tf_op jit(solution)/shard_map/dot_general | solution.py:104
  34.9 54.5 %all-gather.5.cloned.1.call-done = bf16[64,256,48]{1,2,0:T(8,128)(2,1)} async-done(((bf16[2,256,48]{1,2,0:T(8,128)(2,1)}), bf16[64,256,48]{1,2,0:T(8,128)(2,1)}) %all-gather.5.cloned.1.call-update) | async-done | bytes 1572880 | tf_op jit(solution)/shard_map/all_gather | solution.py:85
  89.4 2.0 gather_fusion.2
  92.9 25.7 %all-reduce.1 = bf16[1024,48]{0,1:T(8,128)(2,1)S(1)} all-reduce(f32[1024,48]{0,1:T(8,128)S(1)} %multiply_reduce_fusion), channel_id=1, replica_groups=mesh['grp'=32,'tp'=8] {'tp'}, use_global_device_ids=true, to_apply=%region_4.5 | all-reduce | flops 49152 | bytes 294912 | tf_op jit(solution)/shard_map/psum | solution.py:100
  118.6 47.8 %all-gather.3.cloned.1.call-done = bf16[64,3,16,256]{3,2,1,0:T(8,128)(2,1)} async-done(((bf16[2,3,16,256]{3,2,1,0:T(8,128)(2,1)}), bf16[64,3,16,256]{3,2,1,0:T(8,128)(2,1)}) %all-gather.3.cloned.1.call-update) | async-done | bytes 1572880 | tf_op jit(solution)/shard_map/all_gather | solution.py:86
  166.4 2.0 gather_fusion.1
  168.4 2.6 bitcast_add_fusion
  174.3 3.5 collective-permute-start
  177.8 1.6 copy.55
  179.3 1.6 multiply_subtract_fusion
  182.3 3.2 collective-permute-start.1
  186.8 2.6 subtract_convert_fusion
  189.4 7.9 %collective-permute-done.1 = bf16[1024,256]{0,1:T(8,128)(2,1)} collective-permute-done((bf16[1024,256]{0,1:T(8,128)(2,1)}, bf16[1024,256]{0,1:T(8,128)(2,1)}, u32[]{:S(2)}, u32[]{:S(2)}) %collective-permute-start.1) | collective-permute-done | bytes 524320 | tf_op jit(solution)/shard_map/ppermute | solution.py:19
  198.6 10.8 %fusion.53 = (f32[2,1024]{1,0:T(2,128)S(1)}, f32[2,1024,2048]{2,1,0:T(8,128)}) fusion(pred[1024,2048]{1,0:T(8,128)(4,1)} %pad_add_fusion, bf16[1024,2,128]{2,0,1:T(8,128)(2,1)S(1)} %maximum_convert_fusion, bf16[1024,2,128]{2,0,1:T(8,128)(2,1)S(1)} %copy.45, bf16[1024,2,64]{2,0,1:T(8,128)(2,1)} %get-tuple-element.7, bf16[1024,2,64]{2,0,1:T(8,128)(2,1)} %get-tuple-element.6), kind=kOutput, calls=%fused_computation.109 | convolution fusion | flops 1093666816 | bytes 20455424 | tf_op jit(solution)/shard_map/sub | solution.py:132
  209.3 8.9 %fusion.17 = bf16[2,128,1024]{2,1,0:T(8,128)(2,1)S(1)} fusion(f32[2,1024,2048]{2,1,0:T(8,128)} %get-tuple-element.17, f32[2,1024]{1,0:T(2,128)S(1)} %get-tuple-element.16, bf16[1024,2,128]{0,2,1:T(8,128)(2,1)S(1)} %slice_bitcast_fusion, bf16[1024,2,128]{0,2,1:T(8,128)(2,1)} %bitcast.17), kind=kOutput, calls=%fused_computation.33 | convolution fusion | flops 1084489728 | bytes 18358272 | tf_op jit(solution)/shard_map/hts,shd->thd/dot_general | solution.py:134
  219.1 3.2 convolution_convert_fusion
  222.4 49.4 %all_gather.14 = bf16[64,256,16]{1,2,0:T(8,128)(2,1)S(1)} all-gather(bf16[2,256,16]{1,2,0:T(8,128)(2,1)S(1)} %copy-done.7), channel_id=1, replica_groups=mesh['grp'=32,'tp'=8] {'grp'}, dimensions={0}, use_global_device_ids=true | all-gather | bytes 540672 | tf_op jit(solution)/shard_map/all_gather | solution.py:87
  272.4 48.5 %all_gather.15 = bf16[64,16,256]{2,1,0:T(8,128)(2,1)S(1)} all-gather(bf16[2,16,256]{2,1,0:T(8,128)(2,1)S(1)} %copy-done.8), channel_id=1, replica_groups=mesh['grp'=32,'tp'=8] {'grp'}, dimensions={0}, use_global_device_ids=true | all-gather | bytes 540672 | tf_op jit(solution)/shard_map/all_gather | solution.py:88
  326.1 23.6 %psum.15 = bf16[1024,16]{0,1:T(8,128)(2,1)S(1)} all-reduce(bf16[1024,16]{0,1:T(8,128)(2,1)S(1)} %multiply_reduce_fusion.1), channel_id=1, replica_groups=mesh['grp'=32,'tp'=8] {'tp'}, use_global_device_ids=true, to_apply=%region_10.11 | all-reduce | flops 16384 | bytes 65536 | tf_op jit(solution)/shard_map/psum | solution.py:143
  349.7 2.3 fusion.16
  (78 shorter events, 23.7 us)
Async XLA Ops:
  7.2 211.9 %copy-start = (bf16[256,2048]{1,0:T(8,128)(2,1)S(1)}, bf16[256,2048]{1,0:T(8,128)(2,1)}, u32[]{:S(2)}) copy-start(bf16[256,2048]{1,0:T(8,128)(2,1)} %param.15) | copy-start | bytes 3145732
  7.2 82.2 %all-gather.5.cloned.1.call-start = ((), (), s32[]{:S(2)}) async-start(), calls=%async_computation.2 | async-start | bytes 1622016 | tf_op jit(solution)/shard_map/all_gather | solution.py:85
  7.9 158.5 %all-gather.3.cloned.1.call-start = ((), (), s32[]{:S(2)}) async-start(), calls=%async_computation.1 | async-start | bytes 1622016 | tf_op jit(solution)/shard_map/all_gather | solution.py:86
  8.7 341.0 %reduce-scatter.2.cloned.1.call-start = ((), (), s32[]{:S(2)}) async-start(), calls=%async_computation.3 | async-start | bytes 4718592 | tf_op jit(solution)/shard_map/reduce_scatter | solution.py:139
  22.3 4.6 %copy-start.9 = (f32[2048]{0:T(1024)S(1)}, f32[2048]{0:T(1024)}, u32[]{:S(2)}) copy-start(f32[2048]{0:T(1024)} %param.13) | copy-start | bytes 24580
  22.3 4.6 %copy-start.1 = (bf16[1024,2048]{1,0:T(8,128)(2,1)S(1)}, bf16[1024,2048]{1,0:T(8,128)(2,1)}, u32[]{:S(2)}) copy-start(bf16[1024,2048]{1,0:T(8,128)(2,1)} %param.12) | copy-start | bytes 12582916
  26.8 3.0 copy-start.5
  27.9 1.9 copy-start.3
  171.0 1.8 copy-start.2
  174.3 35.1 %collective-permute-start = (bf16[1024,256]{0,1:T(8,128)(2,1)}, bf16[1024,256]{0,1:T(8,128)(2,1)}, u32[]{:S(2)}, u32[]{:S(2)}) collective-permute-start(bf16[1024,256]{0,1:T(8,128)(2,1)} %bitcast.83), channel_id=1, source_target_pairs={{0,8},{8,16},{16,24},{24,32},{32,40},{40,48},{48,56},{56,64},{64,7... | collective-permute-start | bytes 1572872 | tf_op jit(solution)/shard_map/ppermute | solution.py:19
  182.3 14.9 %collective-permute-start.1 = (bf16[1024,256]{0,1:T(8,128)(2,1)}, bf16[1024,256]{0,1:T(8,128)(2,1)}, u32[]{:S(2)}, u32[]{:S(2)}) collective-permute-start(bf16[1024,256]{0,1:T(8,128)(2,1)} %bitcast.24), channel_id=1, source_target_pairs={{0,8},{8,16},{16,24},{24,32},{32,40},{40,48},{48,56},{56,64},{64,7... | collective-permute-start | bytes 1572872 | tf_op jit(solution)/shard_map/ppermute | solution.py:19
  218.3 0.8 copy-start.4
  219.1 3.3 copy-start.7
  222.3 50.0 %copy-start.8 = (bf16[2,16,256]{2,1,0:T(8,128)(2,1)S(1)}, bf16[2,16,256]{2,1,0:T(8,128)(2,1)}, u32[]{:S(2)}) copy-start(bf16[2,16,256]{2,1,0:T(8,128)(2,1)} %param.19) | copy-start | bytes 49156
  222.3 99.1 %copy-start.10 = (s32[1,8]{1,0:T(1,128)S(1)}, s32[1,8]{1,0:T(1,128)}, u32[]{:S(2)}) copy-start(s32[1,8]{1,0:T(1,128)} %param.23) | copy-start | bytes 100
  222.3 99.8 %copy-start.6 = (bf16[1024,1,2,128]{0,3,2,1:T(8,128)(2,1)S(1)}, bf16[1024,1,2,128]{0,3,2,1:T(8,128)(2,1)}, u32[]{:S(2)}) copy-start(bf16[1024,1,2,128]{0,3,2,1:T(8,128)(2,1)} %slice.61) | copy-start | bytes 1572868
Sparse Core Ops, SparseCore 0:
  10.6 78.7 all-gather.4
  92.0 74.4 all-gather.2
  222.5 41.1 reduce-scatter.1
where the time goes:
time: 359 us
  blocking collectives  147 us (41%)
  waiting for transfers between devices  112 us (31%)
  matrix products  35.6 us (10%)
  local copies, waits for them, and re-layouts  25.7 us (7%)
  other arithmetic  16.4 us (5%)
  between operations  15.4 us (4%)
  starting transfers between devices  6.77 us (2%)
    all_gather x1, waiting for transfers between devices, local(): lax.all_gather(a_in, 'grp', axis=0, tiled=True)  54.5 us
    all_gather x1, blocking collectives, local(): lax.all_gather(a_out, 'grp', axis=0, tiled=True)  49.4 us
    all_gather x1, blocking collectives, local(): lax.all_gather(b_out, 'grp', axis=0, tiled=True)  48.5 us
    all_gather x1, waiting for transfers between devices, local(): lax.all_gather(b_in, 'grp', axis=0, tiled=True)  47.8 us
    psum x1, blocking collectives, local(): lowrank_f = lax.psum(jnp.sum(down_f * member_f[:, :, None], axis=1), 'tp')  25.7 us
    psum x1, blocking collectives, local(): lax.psum(jnp.sum(down_o * member_f[:, :, None], axis=1).astype(jnp.bfloat...  23.6 us
    sub x1, matrix products, local(): weights = jnp.exp(scores - row_top)  10.8 us
    unnamed x27, local copies, waits for them, and re-layouts  10.4 us
  transfers between devices with their start and end apart: 5, of which 3 were waited for; matrix products, arithmetic and copies ran while one was open for 15% of the time, Pallas kernels for 0%

commit v1 on v0

--- a/solution.py
+++ b/solution.py
@@ -17,6 +17,44 @@
     devices = range(lax.axis_size(axis))
     route = [(i - distance, i) for i in devices if i - distance in devices]
     return lax.ppermute(block, axis, route)
+
+
+USED = 16
+
+
+def xor_allreduce(value, axis):
+    count = lax.axis_size(axis)
+    step = 1
+    while step < count:
+        route = [(i, i ^ step) for i in range(count)]
+        value = value + lax.ppermute(value, axis, route)
+        step *= 2
+    return value
+
+
+def fetch_adapters(stores, req_adapter, holder, wanted, group_id):
+    held = stores[0].shape[0]
+    total = holder.shape[0]
+    names = jnp.arange(total, dtype=jnp.int32)
+    used = jnp.any(req_adapter.reshape(-1)[:, None] == names[None, :], axis=0)
+    rank = jnp.cumsum(used.astype(jnp.int32)) - 1
+    picks = jnp.arange(USED, dtype=jnp.int32)
+    hit = used[None, :] & (rank[None, :] == picks[:, None])
+    chosen = jnp.sum(jnp.where(hit, names[None, :], 0), axis=1)
+    slots = holder[chosen]
+    mine = (slots // held) == group_id
+    local_idx = slots % held
+    flat = jnp.concatenate([s.reshape(held, -1) for s in stores], axis=1)
+    compact = jnp.where(mine[:, None], jnp.take(flat, local_idx, axis=0), jnp.zeros((), flat.dtype))
+    compact = lax.psum(compact, "grp")
+    mine_rows = jnp.take(compact, rank[wanted], axis=0)
+    out = []
+    at = 0
+    for s in stores:
+        size = math.prod(s.shape[1:])
+        out.append(mine_rows[:, at : at + size].reshape((wanted.shape[0],) + s.shape[1:]))
+        at += size
+    return tuple(out)
 
 
 def rms_norm(token_rows, norm_gain):
@@ -81,23 +119,15 @@
     offset = jnp.where(continued, prev_len, 0)
     segment, member, position = request_layout(lengths, offset, tok_count)
     wanted = lax.dynamic_index_in_dim(req_adapter, group_id, 0, keepdims=False)
-    stacks = (
-        lax.all_gather(a_in, "grp", axis=0, tiled=True),
-        lax.all_gather(b_in, "grp", axis=0, tiled=True),
-        lax.all_gather(a_out, "grp", axis=0, tiled=True),
-        lax.all_gather(b_out, "grp", axis=0, tiled=True),
-    )
-    req_slots = holder[wanted]
-    sel_in = jnp.take(stacks[0], req_slots, axis=0)
-    sel_up = jnp.take(stacks[1], req_slots, axis=0)
-    sel_odown = jnp.take(stacks[2], req_slots, axis=0)
-    sel_oup = jnp.take(stacks[3], req_slots, axis=0)
+    sel_in, sel_up, sel_odown, sel_oup = fetch_adapters(
+        (a_in, b_in, a_out, b_out), req_adapter, holder, wanted, group_id
+    )
     member_f = member.astype(jnp.float32)
     pick_bf = member.astype(jnp.bfloat16)
     normed = rms_norm(tokens, norm_gain)
     own_cols = lax.dynamic_slice_in_dim(normed, tp_id * local_width, local_width, 1)
     down_f = jnp.einsum("td,rdk->trk", own_cols, sel_in, preferred_element_type=jnp.float32)
-    lowrank_f = lax.psum(jnp.sum(down_f * member_f[:, :, None], axis=1), "tp")
+    lowrank_f = xor_allreduce(jnp.sum(down_f * member_f[:, :, None], axis=1), "tp")
     lowrank = lowrank_f.astype(jnp.bfloat16)
     spread = (pick_bf[:, :, None] * lowrank[:, None, :]).reshape(tok_count, req_count, 3, rank_dim)
     delta_qkv = jnp.einsum("trck,rckd->tcd", spread, sel_up, preferred_element_type=jnp.float32)
@@ -136,11 +166,19 @@
     )
     attended = mixed_heads.astype(jnp.bfloat16).reshape(tok_count, local_width)
     partial_value = jnp.dot(attended, w_out, preferred_element_type=jnp.float32)
-    base_out = lax.psum_scatter(
-        partial_value.astype(jnp.bfloat16), "tp", scatter_dimension=1, tiled=True
-    ).astype(jnp.float32)
     down_o = jnp.einsum("td,rdk->trk", attended, sel_odown, preferred_element_type=jnp.float32)
-    low_o = lax.psum(jnp.sum(down_o * member_f[:, :, None], axis=1).astype(jnp.bfloat16), "tp")
+    low_part = jnp.sum(down_o * member_f[:, :, None], axis=1).astype(jnp.bfloat16)
+    n_tp = lax.axis_size("tp")
+    packed = jnp.concatenate(
+        [
+            partial_value.astype(jnp.bfloat16).reshape(tok_count, n_tp, local_width),
+            jnp.broadcast_to(low_part[:, None, :], (tok_count, n_tp, rank_dim)),
+        ],
+        axis=2,
+    ).reshape(tok_count, n_tp * (local_width + rank_dim))
+    summed = lax.psum_scatter(packed, "tp", scatter_dimension=1, tiled=True)
+    base_out = summed[:, :local_width].astype(jnp.float32)
+    low_o = summed[:, local_width:]
     spread_o = (pick_bf[:, :, None] * low_o[:, None, :]).reshape(tok_count, req_count * rank_dim)
     delta_o = jnp.dot(
         spread_o,

time: 359 us -> 314 us (0.87)
  blocking collectives: 147 us -> 0 us
  waiting for transfers between devices: 112 us -> 183 us
  local copies, waits for them, and re-layouts: 25.7 us -> 40.9 us
  other arithmetic: 16.4 us -> 26.4 us
  starting transfers between devices: 6.77 us -> 11.4 us
    psum x0 -> x1, waiting for transfers between devices: none -> 129 us  [fetch_adapters(): compact = lax.psum(compact, 'grp')]
    all_gather x2 -> x0, waiting for transfers between devices: 102 us -> none  [the longest x1 54.5 us: local(): lax.all_gather(a_in, 'grp', axis=0, tiled=True)]
    all_gather x2 -> x0, blocking collectives: 97.9 us -> none  [the longest x1 49.4 us: local(): lax.all_gather(a_out, 'grp', axis=0, tiled=True)]
    psum x2 -> x0, blocking collectives: 49.3 us -> none  [the longest x1 25.7 us: local(): lowrank_f = lax.psum(jnp.sum(down_f * member_f[:, :, None], axis=1), 'tp')]
    unnamed x3, waiting for transfers between devices: 1.39 us -> 36.3 us
    reshape x0 -> x7, local copies, waits for them, and re-layouts: none -> 7.49 us  [the longest x1 6.42 us: local(): partial_value.astype(jnp.bfloat16).reshape(tok_count, n_tp, local_width)]
    ppermute x0 -> x3, waiting for transfers between devices: none -> 6.53 us  [xor_allreduce(): value = value + lax.ppermute(value, axis, route)]
    ppermute x0 -> x3, starting transfers between devices: none -> 4.94 us  [xor_allreduce(): value = value + lax.ppermute(value, axis, route)]
  transfers between devices with their start and end apart: 5 -> 7, of which waited for: 3 -> 5; matrix products, arithmetic and copies ran while one was open for 15% -> 16% of each run, Pallas kernels for 0% -> 0%
where the time goes in v1:
time: 314 us; the launch traced here: 312 us
  waiting for transfers between devices  183 us (58%)
  local copies, waits for them, and re-layouts  40.9 us (13%)
  matrix products  34.3 us (11%)
  other arithmetic  26.4 us (8%)
  between operations  15.9 us (5%)
  starting transfers between devices  11.4 us (4%)
    psum x1, waiting for transfers between devices, fetch_adapters(): compact = lax.psum(compact, 'grp')  129 us
    unnamed x3, waiting for transfers between devices  36.3 us
    unnamed x34, local copies, waits for them, and re-layouts  15.3 us
    ppermute x2, waiting for transfers between devices, shifted(): return lax.ppermute(block, axis, route)  11.2 us
    sub x1, matrix products, local(): weights = jnp.exp(scores - row_top)  10.8 us
    dot_general x1, matrix products, local(): jnp.einsum('hts,shd->thd', weights_bf, value_all, preferred_element_type=...  8.93 us
    ppermute x3, waiting for transfers between devices, xor_allreduce(): value = value + lax.ppermute(value, axis, route)  6.53 us
    reshape x1, local copies, waits for them, and re-layouts, local(): partial_value.astype(jnp.bfloat16).reshape(tok_count, n_tp, local_width)  6.42 us
  transfers between devices with their start and end apart: 7, of which 5 were waited for; matrix products, arithmetic and copies ran while one was open for 16% of the time, Pallas kernels for 0%

profile of v1, /device:TPU:2, one launch (start us, length us, event | category | flops | bytes accessed | tf_op | source)
XLA Modules:
  0.0 312.4 jit_solution(5977130857267515130)
XLA Ops:
  19.6 3.1 fusion.2
  23.4 4.7 %copy.62 = bf16[2048,3,256]{0,2,1:T(8,128)(2,1)} copy(bf16[2048,3,256]{2,0,1:T(8,128)(2,1)} %param.14) | data formatting | bytes 6291456 | tf_op args[2]
  28.6 3.5 %fusion.4 = bf16[1024,2048]{1,0:T(8,128)(2,1)S(1)} fusion(bf16[1024,2048]{1,0:T(8,128)(2,1)} %param.12, f32[2048]{0:T(1024)S(1)} %copy-done.7, f32[1024]{0:T(1024)S(1)} %add_rsqrt_fusion), kind=kLoop, calls=%fused_computation.14 | loop fusion | flops 8388608 | bytes 8400896 | tf_op jit(solution)/shard_map/convert_element_type | solution.py:63
  32.2 1.9 copy-done.2
  34.1 5.1 %fusion.9 = f32[1024,3,256]{0,2,1:T(8,128)} fusion(bf16[1024,2048]{1,0:T(8,128)(2,1)S(1)} %fusion.4, bf16[2048,3,256]{0,2,1:T(8,128)(2,1)S(1)} %copy-done.3), kind=kOutput, calls=%fused_computation.21 | convolution fusion | flops 3221225472 | bytes 10485760 | tf_op jit(solution)/shard_map/dot_general | solution.py:134
  39.2 129.4 %all-reduce.2.cloned.1.call-done = bf16[16,32768]{1,0:T(8,128)(2,1)} async-done(((bf16[16,32768]{1,0:T(8,128)(2,1)}), bf16[16,32768]{1,0:T(8,128)(2,1)}) %all-reduce.2.cloned.1.call-update) | async-done | bytes 1048592 | tf_op jit(solution)/shard_map/psum | solution.py:49
  168.6 2.4 gather_fusion.3
  177.7 3.0 multiply_cosine_fusion
  180.7 2.8 collective-permute-done.1
  183.5 3.3 %collective-permute-start.2 = (f32[1024,48]{0,1:T(8,128)S(1)}, f32[1024,48]{0,1:T(8,128)S(1)}, u32[]{:S(2)}, u32[]{:S(2)}) collective-permute-start(f32[1024,48]{0,1:T(8,128)S(1)} %add.163), channel_id=1, source_target_pairs={{0,4},{1,5},{2,6},{3,7},{4,0},{5,1},{6,2},{7,3},{8,12},{9,13},{10,... | collective-permute-start | bytes 589832 | tf_op jit(solution)/shard_map/ppermute | solution.py:30
  188.0 3.7 %collective-permute-done.2 = f32[1024,48]{0,1:T(8,128)S(1)} collective-permute-done((f32[1024,48]{0,1:T(8,128)S(1)}, f32[1024,48]{0,1:T(8,128)S(1)}, u32[]{:S(2)}, u32[]{:S(2)}) %collective-permute-start.2) | collective-permute-done | bytes 196640 | tf_op jit(solution)/shard_map/ppermute | solution.py:30
  191.7 2.5 bitcast_add_fusion
  197.6 3.0 collective-permute-start.3
  202.1 1.6 multiply_subtract_fusion
  205.1 3.4 %collective-permute-start.4 = (bf16[1024,256]{0,1:T(8,128)(2,1)}, bf16[1024,256]{0,1:T(8,128)(2,1)}, u32[]{:S(2)}, u32[]{:S(2)}) collective-permute-start(bf16[1024,256]{0,1:T(8,128)(2,1)} %bitcast.29), channel_id=1, source_target_pairs={{0,8},{8,16},{16,24},{24,32},{32,40},{40,48},{48,56},{56,64},{64,7... | collective-permute-start | bytes 1572872 | tf_op jit(solution)/shard_map/ppermute | solution.py:19
  209.8 2.6 subtract_convert_fusion
  212.4 11.2 %collective-permute-done.4 = bf16[1024,256]{0,1:T(8,128)(2,1)} collective-permute-done((bf16[1024,256]{0,1:T(8,128)(2,1)}, bf16[1024,256]{0,1:T(8,128)(2,1)}, u32[]{:S(2)}, u32[]{:S(2)}) %collective-permute-start.4) | collective-permute-done | bytes 524320 | tf_op jit(solution)/shard_map/ppermute | solution.py:19
  224.9 10.8 %fusion.49 = (f32[2,1024]{1,0:T(2,128)S(1)}, f32[2,1024,2048]{2,1,0:T(8,128)}) fusion(pred[1024,2048]{1,0:T(8,128)(4,1)} %pad_add_fusion, bf16[1024,2,128]{2,0,1:T(8,128)(2,1)S(1)} %maximum_convert_fusion, bf16[1024,2,128]{2,0,1:T(8,128)(2,1)S(1)} %copy.72, bf16[1024,2,64]{2,0,1:T(8,128)(2,1)} %get-tuple-element.7, bf16[1024,2,64]{2,0,1:T(8,128)(2,1)} %get-tuple-element.6), kind=kOutput, calls=%fused_computation.127 | convolution fusion | flops 1093666816 | bytes 20455424 | tf_op jit(solution)/shard_map/sub | solution.py:162
  235.7 8.9 %fusion.16 = bf16[2,128,1024]{2,1,0:T(8,128)(2,1)S(1)} fusion(f32[2,1024,2048]{2,1,0:T(8,128)} %get-tuple-element.23, f32[2,1024]{1,0:T(2,128)S(1)} %get-tuple-element.22, bf16[1024,2,128]{0,2,1:T(8,128)(2,1)S(1)} %slice_bitcast_fusion, bf16[1024,2,128]{0,2,1:T(8,128)(2,1)} %bitcast.22), kind=kOutput, calls=%fused_computation.32 | convolution fusion | flops 1084489728 | bytes 18358272 | tf_op jit(solution)/shard_map/hts,shd->thd/dot_general | solution.py:164
  244.9 3.2 %convolution_convert_fusion = bf16[1024,2048]{1,0:T(8,128)(2,1)} fusion(bf16[1024,256]{0,1:T(8,128)(2,1)S(1)} %bitcast.104, bf16[256,2048]{1,0:T(8,128)(2,1)S(1)} %copy-done), kind=kOutput, calls=%fused_computation.25 | convolution fusion | flops 1075838976 | bytes 5767168 | tf_op jit(solution)/shard_map/dot_general | solution.py:168
  248.1 6.4 %copy.82 = bf16[1024,2048]{0,1:T(8,128)(2,1)} copy(bf16[1024,2048]{1,0:T(8,128)(2,1)} %convolution_convert_fusion) | data formatting | bytes 8388608 | tf_op jit(solution)/shard_map/reshape | solution.py:174
  254.6 4.7 %pad_maximum_fusion = bf16[1024,8,272]{0,2,1:T(8,128)(2,1)} fusion(bf16[1024,8,16]{0,2,1:T(8,128)(2,1)S(1)} %broadcast_in_dim.158, bf16[1024,8,256]{0,2,1:T(8,128)(2,1)} %bitcast.97), kind=kLoop, calls=%fused_computation.20 | loop fusion | flops 8912896 | bytes 8912896 | tf_op jit(solution)/shard_map/concatenate | solution.py:172
  265.1 36.3 %reduce-scatter.4.cloned.1.call-done = bf16[272,1024]{1,0:T(8,128)(2,1)} async-done(((bf16[2176,1024]{1,0:T(8,128)(2,1)}), bf16[272,1024]{1,0:T(8,128)(2,1)}) %reduce-scatter.4.cloned.1.call-update) | async-done | bytes 557072
  303.4 2.2 fusion.15
  (114 shorter events, 36.8 us)
Async XLA Ops:
  7.2 237.7 %copy-start = (bf16[256,2048]{1,0:T(8,128)(2,1)S(1)}, bf16[256,2048]{1,0:T(8,128)(2,1)}, u32[]{:S(2)}) copy-start(bf16[256,2048]{1,0:T(8,128)(2,1)} %param.15) | copy-start | bytes 3145732
  7.2 161.5 %all-reduce.2.cloned.1.call-start = ((), (), s32[]{:S(2)}) async-start(), calls=%async_computation.1 | async-start | bytes 2097152 | tf_op jit(solution)/shard_map/psum | solution.py:49
  14.0 2.5 copy-start.8
  14.0 2.5 copy-start.9
  16.4 284.9 %reduce-scatter.4.cloned.1.call-start = ((), (), s32[]{:S(2)}) async-start(), calls=%async_computation.2 | async-start | bytes 5013504
  22.7 5.9 %copy-start.7 = (f32[2048]{0:T(1024)S(1)}, f32[2048]{0:T(1024)}, u32[]{:S(2)}) copy-start(f32[2048]{0:T(1024)} %param.13) | copy-start | bytes 24580
  28.6 5.4 %copy-start.3 = (bf16[2048,3,256]{0,2,1:T(8,128)(2,1)S(1)}, bf16[2048,3,256]{0,2,1:T(8,128)(2,1)}, u32[]{:S(2)}) copy-start(bf16[2048,3,256]{0,2,1:T(8,128)(2,1)} %copy.62) | copy-start | bytes 9437188
  32.1 1.9 copy-start.2
  171.2 0.7 copy-start.5
  173.0 14.6 %copy-start.6 = (bf16[4,12288]{1,0:T(4,128)(2,1)S(1)}, bf16[4,12288]{1,0:T(4,128)(2,1)}, u32[]{:S(2)}) copy-start(bf16[4,12288]{1,0:T(4,128)(2,1)} %get-tuple-element.13) | copy-start | bytes 294916
  174.5 1.6 collective-permute-start
  176.1 7.4 %collective-permute-start.1 = (f32[1024,48]{0,1:T(8,128)S(1)}, f32[1024,48]{0,1:T(8,128)S(1)}, u32[]{:S(2)}, u32[]{:S(2)}) collective-permute-start(f32[1024,48]{0,1:T(8,128)S(1)} %add.162), channel_id=1, source_target_pairs={{0,2},{1,3},{2,0},{3,1},{4,6},{5,7},{6,4},{7,5},{8,10},{9,11},{10,... | collective-permute-start | bytes 589832 | tf_op jit(solution)/shard_map/ppermute | solution.py:30
  183.5 8.2 %collective-permute-start.2 = (f32[1024,48]{0,1:T(8,128)S(1)}, f32[1024,48]{0,1:T(8,128)S(1)}, u32[]{:S(2)}, u32[]{:S(2)}) collective-permute-start(f32[1024,48]{0,1:T(8,128)S(1)} %add.163), channel_id=1, source_target_pairs={{0,4},{1,5},{2,6},{3,7},{4,0},{5,1},{6,2},{7,3},{8,12},{9,13},{10,... | collective-permute-start | bytes 589832 | tf_op jit(solution)/shard_map/ppermute | solution.py:30
  194.2 1.8 copy-start.1
  197.6 38.1 %collective-permute-start.3 = (bf16[1024,256]{0,1:T(8,128)(2,1)}, bf16[1024,256]{0,1:T(8,128)(2,1)}, u32[]{:S(2)}, u32[]{:S(2)}) collective-permute-start(bf16[1024,256]{0,1:T(8,128)(2,1)} %bitcast.106), channel_id=1, source_target_pairs={{0,8},{8,16},{16,24},{24,32},{32,40},{40,48},{48,56},{56,64},{64,7... | collective-permute-start | bytes 1572872 | tf_op jit(solution)/shard_map/ppermute | solution.py:19
  205.1 18.5 %collective-permute-start.4 = (bf16[1024,256]{0,1:T(8,128)(2,1)}, bf16[1024,256]{0,1:T(8,128)(2,1)}, u32[]{:S(2)}, u32[]{:S(2)}) collective-permute-start(bf16[1024,256]{0,1:T(8,128)(2,1)} %bitcast.29), channel_id=1, source_target_pairs={{0,8},{8,16},{16,24},{24,32},{32,40},{40,48},{48,56},{56,64},{64,7... | collective-permute-start | bytes 1572872 | tf_op jit(solution)/shard_map/ppermute | solution.py:19
  259.3 0.7 copy-start.10
  259.3 1.3 copy-start.4
Sparse Core Ops, SparseCore 0:
  16.6 152.0 all-reduce.1
  259.4 41.8 reduce-scatter.3
